TPU v7x, 256 devices: a whole 4x4x8 slice. The times are simulated.
256 devices in a mesh: expert: 16 (over z, core), fsdp: 16 (over x, y).
Axes of the slice: x: 4, y: 4, z: 8, core: 2. Of those that a mesh axis runs over, the one named last changes fastest.
Arguments:
- tokens: bfloat16 [4096, 6144], P(('expert', 'fsdp')), may hold values from -6 to 6
- expert_ids: int32 [4096, 4], P(('expert', 'fsdp')), may hold values from 0 to 15, all different within a row; in each aligned block of 16 rows (0 to 15, 16 to 31, ...) at most 5 rows name the same one
- router_weight: float32 [4096, 4], P(('expert', 'fsdp')), may hold values from 0.1 to 1
- w_gate: bfloat16 [16, 5376, 6144], P('expert', 'fsdp'), may hold values from -0.078125 to 0.078125
- w_up: bfloat16 [16, 5376, 6144], P('expert', 'fsdp'), may hold values from -0.078125 to 0.078125
Outputs:
- routed: bfloat16 [4096, 4, 5376], P(('expert', 'fsdp'))
Inputs may be any that keep to these rules, and one draw needn't show every extreme that they name: `expert_ids`: each row names 4 different experts; the 16 rows of one device name any one expert at most 5 times, and some device names some expert exactly 5 times.
All inputs are finite; a program needn't handle non-finite values.
Results may differ from a plain program's by a relative error of at most 0.0049.
Values may be sent and summed in bfloat16 or wider, within the bound.
No kernel may reach another device: no remote copies, remote signals or barrier semaphores. Data moves between devices by JAX's collectives and lax.ppermute only.
A program may use at most 128 MiB of HBM per device.

v0:
```python
import jax
import jax.numpy as jnp
from jax import lax
from jax.sharding import PartitionSpec as P


def hidden_block(row_block, gate_rows, up_rows):
    gate_act = lax.dot_general(
        row_block, gate_rows, (((1,), (1,)), ((), ())), preferred_element_type=jnp.float32
    )
    up_act = lax.dot_general(
        row_block, up_rows, (((1,), (1,)), ((), ())), preferred_element_type=jnp.float32
    )
    return (jax.nn.gelu(gate_act, approximate=False) * up_act).astype(jnp.bfloat16)


def local(tokens, expert_ids, router_weight, w_gate, w_up):
    tok_rows, model_width = tokens.shape
    top_count = expert_ids.shape[1]
    experts = lax.axis_size("expert")
    fsdp_size = lax.axis_size("fsdp")
    cap_slots = 5 * tok_rows * top_count // (4 * experts)
    flat_ids = expert_ids.reshape(-1)
    choosing = (flat_ids[:, None] == jnp.arange(experts, dtype=jnp.int32)[None, :]).astype(
        jnp.int32
    )
    slot_rank = jnp.sum((jnp.cumsum(choosing, axis=0) - 1) * choosing, axis=1)
    slot_of = flat_ids * cap_slots + slot_rank
    placing = (
        slot_of[None, :] == jnp.arange(experts * cap_slots, dtype=jnp.int32)[:, None]
    ).astype(jnp.bfloat16)
    repeated = jnp.repeat(tokens, top_count, axis=0)
    outgoing = jnp.dot(placing, repeated, preferred_element_type=jnp.float32).astype(jnp.bfloat16)
    outgoing = outgoing.reshape(experts, cap_slots, model_width)
    gate_rows = w_gate[0]
    up_rows = w_up[0]
    columns = gate_rows.shape[0]
    arrived = lax.all_to_all(outgoing, "expert", split_axis=0, concat_axis=0, tiled=True)
    local_hidden = hidden_block(
        lax.all_gather(arrived.reshape(-1, model_width), "fsdp", axis=0, tiled=True),
        gate_rows,
        up_rows,
    )
    shaped = local_hidden.reshape(fsdp_size, experts, cap_slots, columns)
    by_owner = jnp.transpose(shaped, (1, 0, 2, 3)).reshape(experts * fsdp_size, cap_slots, columns)
    returned = lax.all_to_all(by_owner, ("expert", "fsdp"), 0, 0, tiled=True)
    returned = returned.reshape(experts, fsdp_size, cap_slots, columns)
    returned = jnp.transpose(returned, (0, 2, 1, 3)).reshape(experts * cap_slots, -1)
    collected = lax.dot_general(
        placing, returned, (((0,), (0,)), ((), ())), preferred_element_type=jnp.float32
    )
    routed = (router_weight.reshape(-1, 1) * collected).astype(jnp.bfloat16)
    return routed.reshape(tok_rows, top_count, -1)


def solution(mesh):
    return jax.shard_map(
        local,
        mesh=mesh,
        in_specs=(
            P(("expert", "fsdp"), None),
            P(("expert", "fsdp"), None),
            P(("expert", "fsdp"), None),
            P("expert", "fsdp", None),
            P("expert", "fsdp", None),
        ),
        out_specs=P(("expert", "fsdp"), None, None),
        check_vma=False,
    )
```

profile of v0, /device:TPU:8, one launch (start us, length us, event | category | flops | bytes accessed | tf_op | source)
XLA Modules:
  0.0 256.1 jit_solution(8228887948077420177)
XLA Ops:
  6.5 0.8 copy.14
  7.5 0.1 reduce_window_sum.11
  7.6 0.2 select_reduce_fusion
  7.8 1.2 broadcast_in_dim.2
  9.0 0.2 reshape.39
  9.2 0.4 convolution_convert_fusion
  9.6 0.5 reshape.40
  10.1 46.9 %all_to_all.10 = bf16[16,5,6144]{2,1,0:T(8,128)(2,1)S(1)} all-to-all(bf16[16,5,6144]{2,1,0:T(8,128)(2,1)S(1)} %reshape.40), channel_id=1, replica_groups=mesh['expert'=16,'fsdp'=16] {'expert'}, dimensions={0} | all-to-all | bytes 1966080 | tf_op jit(solution)/shard_map/all_to_all | solution.py:38
  56.9 1.2 reshape.41
  58.2 109.6 %all-gather.2.cloned.1.call-done = bf16[1280,6144]{1,0:T(8,128)(2,1)} async-done(((bf16[80,6144]{1,0:T(8,128)(2,1)}), bf16[1280,6144]{1,0:T(8,128)(2,1)}) %all-gather.2.cloned.1.call-update) | async-done | bytes 15728656 | tf_op jit(solution)/shard_map/all_gather | solution.py:40
  167.8 11.7 %fusion.3 = f32[1280,336]{0,1:T(8,128)S(1)} fusion(bf16[1280,6144]{1,0:T(8,128)(2,1)} %all-gather.2.cloned.1.call-done, bf16[1,336,6144]{2,1,0:T(8,128)(2,1)} %param.8), kind=kOutput, calls=%fused_computation.5 | convolution fusion | flops 5284823040 | bytes 21577728 | tf_op jit(solution)/shard_map/dot_general | solution.py:8
  179.6 0.5 copy-done.2
  180.1 8.9 %fusion.8 = bf16[1280,336]{0,1:T(8,128)(2,1)S(1)} fusion(bf16[1280,6144]{1,0:T(8,128)(2,1)S(1)} %copy-done.1, bf16[1,336,6144]{2,1,0:T(8,128)(2,1)S(1)} %copy-done.2, f32[1280,336]{0,1:T(8,128)S(1)} %fusion.3), kind=kOutput, calls=%fused_computation.8 | convolution fusion | flops 5313208320 | bytes 22437888 | tf_op jit(solution)/shard_map/dot_general | solution.py:11
  189.0 0.6 copy.15
  189.7 0.7 reshape.42
  190.3 0.7 copy.16
  191.0 1.8 copy.17
  192.8 11.5 %all-to-all-start.1 = ((bf16[256,5,336]{2,1,0:T(8,128)(2,1)}), bf16[256,5,336]{2,1,0:T(8,128)(2,1)S(1)}, u32[]{:S(2)}, u32[]{:S(2)}) async-start(bf16[256,5,336]{2,1,0:T(8,128)(2,1)} %copy.17), calls=%async_computation.1 | async-start | bytes 3145728 | tf_op jit(solution)/shard_map/all_to_all | solution.py:46
  204.5 0.1 mul.41
  204.6 42.0 %all-to-all-done.1 = bf16[256,5,336]{2,1,0:T(8,128)(2,1)S(1)} async-done(((bf16[256,5,336]{2,1,0:T(8,128)(2,1)}), bf16[256,5,336]{2,1,0:T(8,128)(2,1)S(1)}, u32[]{:S(2)}, u32[]{:S(2)}) %all-to-all-start.1) | async-done | bytes 860192 | tf_op jit(solution)/shard_map/all_to_all | solution.py:46
  246.5 0.1 copy.20
  246.7 1.2 reshape.45
  247.9 0.4 fusion
  248.3 1.0 reshape.46
  (11 shorter events, 0.3 us)
Async XLA Ops:
  6.5 161.3 %all-gather.2.cloned.1.call-start = ((), (), s32[]{:S(2)}) async-start(), calls=%async_computation.2 | async-start | bytes 16711680 | tf_op jit(solution)/shard_map/all_gather | solution.py:40
  167.8 11.8 %copy-start.1 = (bf16[1280,6144]{1,0:T(8,128)(2,1)S(1)}, bf16[1280,6144]{1,0:T(8,128)(2,1)}, u32[]{:S(2)}) copy-start(bf16[1280,6144]{1,0:T(8,128)(2,1)} %all-gather.2.cloned.1.call-done) | copy-start | bytes 47185924
  167.8 12.3 %copy-start.2 = (bf16[1,336,6144]{2,1,0:T(8,128)(2,1)S(1)}, bf16[1,336,6144]{2,1,0:T(8,128)(2,1)}, u32[]{:S(2)}) copy-start(bf16[1,336,6144]{2,1,0:T(8,128)(2,1)} %param.9) | copy-start | bytes 12386308
  192.8 11.5 %copy-start = (f32[16,4]{0,1:T(4,128)S(1)}, f32[16,4]{0,1:T(4,128)}, u32[]{:S(2)}) copy-start(f32[16,4]{0,1:T(4,128)} %param.7) | copy-start | bytes 772
  192.8 53.7 %all-to-all-start.1 = ((bf16[256,5,336]{2,1,0:T(8,128)(2,1)}), bf16[256,5,336]{2,1,0:T(8,128)(2,1)S(1)}, u32[]{:S(2)}, u32[]{:S(2)}) async-start(bf16[256,5,336]{2,1,0:T(8,128)(2,1)} %copy.17), calls=%async_computation.1 | async-start | bytes 3145728 | tf_op jit(solution)/shard_map/all_to_all | solution.py:46
Sparse Core Ops, SparseCore 0:
  58.3 109.4 all-gather.1
where the time goes:
time: 256 us
  waiting for transfers between devices  152 us (59%)
  blocking collectives  46.9 us (18%)
  matrix products  21.5 us (8%)
  between operations  13.5 us (5%)
  starting transfers between devices  11.5 us (4%)
  local copies, waits for them, and re-layouts  10.8 us (4%)
    all_gather x1, waiting for transfers between devices, local(): lax.all_gather(arrived.reshape(-1, model_width), 'fsdp', axis=0, tiled=True)  110 us
    all_to_all x1, blocking collectives, local(): lax.all_to_all(outgoing, 'expert', split_axis=0, concat_axis=0, tiled=True)  46.9 us
    all_to_all x1, waiting for transfers between devices, local(): returned = lax.all_to_all(by_owner, ('expert', 'fsdp'), 0, 0, tiled=True)  42 us
    dot_general x1, matrix products, hidden_block(): lax.dot_general(row_block, gate_rows, (((1,), (1,)), ((), ())), preferred...  11.7 us
    all_to_all x1, starting transfers between devices, local(): returned = lax.all_to_all(by_owner, ('expert', 'fsdp'), 0, 0, tiled=True)  11.5 us
    dot_general x1, matrix products, hidden_block(): lax.dot_general(row_block, up_rows, (((1,), (1,)), ((), ())), preferred_e...  8.94 us
  transfers between devices with their start and end apart: 2, of which 2 were waited for; matrix products, arithmetic and copies ran while one was open for 0% of the time, Pallas kernels for 0%

commit v1 on v0

--- a/solution.py
+++ b/solution.py
@@ -2,6 +2,22 @@
 import jax.numpy as jnp
 from jax import lax
 from jax.sharding import PartitionSpec as P
+
+
+def ring_gather(x, axis, dim):
+    ways, here, turn = (lax.axis_size(axis), lax.axis_index(axis), x.shape[dim])
+    lengths = [n * ways if d == dim else n for d, n in enumerate(x.shape)]
+    full = lax.dynamic_update_slice_in_dim(jnp.zeros(lengths, x.dtype), x, here * turn, axis=dim)
+    going_up = going_down = x
+    for far in range(1, ways // 2 + 1):
+        going_up = lax.ppermute(going_up, axis, [(d, (d + 1) % ways) for d in range(ways)])
+        full = lax.dynamic_update_slice_in_dim(full, going_up, (here - far) % ways * turn, axis=dim)
+        if 2 * far < ways:
+            going_down = lax.ppermute(going_down, axis, [(d, (d - 1) % ways) for d in range(ways)])
+            full = lax.dynamic_update_slice_in_dim(
+                full, going_down, (here + far) % ways * turn, axis=dim
+            )
+    return full
 
 
 def hidden_block(row_block, gate_rows, up_rows):
@@ -37,9 +53,7 @@
     columns = gate_rows.shape[0]
     arrived = lax.all_to_all(outgoing, "expert", split_axis=0, concat_axis=0, tiled=True)
     local_hidden = hidden_block(
-        lax.all_gather(arrived.reshape(-1, model_width), "fsdp", axis=0, tiled=True),
-        gate_rows,
-        up_rows,
+        ring_gather(arrived.reshape(-1, model_width), "fsdp", 0), gate_rows, up_rows
     )
     shaped = local_hidden.reshape(fsdp_size, experts, cap_slots, columns)
     by_owner = jnp.transpose(shaped, (1, 0, 2, 3)).reshape(experts * fsdp_size, cap_slots, columns)

time: 256 us -> 334 us (1.30)
  waiting for transfers between devices: 152 us -> 186 us
  starting transfers between devices: 11.5 us -> 41.1 us
  local copies, waits for them, and re-layouts: 10.8 us -> 34.1 us
  between operations: 13.5 us -> 0.16 us
  matrix products: 21.5 us -> 25.3 us
    ppermute x0 -> x15, waiting for transfers between devices: none -> 144 us  [the longest x8 143 us: ring_gather(): lax.ppermute(going_up, axis, [(d, (d + 1) % ways) for d in range(ways)])]
    all_gather x1 -> x0, waiting for transfers between devices: 110 us -> none  [local(): lax.all_gather(arrived.reshape(-1, model_width), 'fsdp', axis=0, tiled=True)]
    ppermute x0 -> x15, starting transfers between devices: none -> 30.7 us  [the longest x7 27.5 us: ring_gather(): lax.ppermute(going_down, axis, [(d, (d - 1) % ways) for d in range(ways)])]
    dynamic_update_slice x0 -> x16, local copies, waits for them, and re-layouts: none -> 16.6 us  [the longest x8 8.24 us: ring_gather(): lax.dynamic_update_slice_in_dim(full, going_up, (here - far) % ways * tur...]
    broadcast_in_dim x0 -> x1, local copies, waits for them, and re-layouts: none -> 7.48 us  [ring_gather(): jnp.zeros(lengths, x.dtype)]
    dot_general x1, matrix products: 8.94 us -> 15.3 us  [hidden_block(): lax.dot_general(row_block, up_rows, (((1,), (1,)), ((), ())), preferred_e...]
  transfers between devices with their start and end apart: 2 -> 16, of which waited for: 2 -> 10; matrix products, arithmetic and copies ran while one was open for 0% -> 7% of each run, Pallas kernels for 0% -> 0%
where the time goes in v1:
time: 334 us
  waiting for transfers between devices  186 us (56%)
  blocking collectives  46.9 us (14%)
  starting transfers between devices  41.1 us (12%)
  local copies, waits for them, and re-layouts  34.1 us (10%)
  matrix products  25.3 us (8%)
    ppermute x8, waiting for transfers between devices, ring_gather(): lax.ppermute(going_up, axis, [(d, (d + 1) % ways) for d in range(ways)])  143 us
    all_to_all x1, blocking collectives, local(): lax.all_to_all(outgoing, 'expert', split_axis=0, concat_axis=0, tiled=True)  46.9 us
    all_to_all x1, waiting for transfers between devices, local(): returned = lax.all_to_all(by_owner, ('expert', 'fsdp'), 0, 0, tiled=True)  42.1 us
    ppermute x7, starting transfers between devices, ring_gather(): lax.ppermute(going_down, axis, [(d, (d - 1) % ways) for d in range(ways)])  27.5 us
    dot_general x1, matrix products, hidden_block(): lax.dot_general(row_block, up_rows, (((1,), (1,)), ((), ())), preferred_e...  15.3 us
    all_to_all x1, starting transfers between devices, local(): returned = lax.all_to_all(by_owner, ('expert', 'fsdp'), 0, 0, tiled=True)  10.3 us
    dot_general x1, matrix products, hidden_block(): lax.dot_general(row_block, gate_rows, (((1,), (1,)), ((), ())), preferred...  9.16 us
    dynamic_update_slice x8, local copies, waits for them, and re-layouts, ring_gather(): lax.dynamic_update_slice_in_dim(full, going_up, (here - far) % ways * tur...  8.24 us
  transfers between devices with their start and end apart: 16, of which 10 were waited for; matrix products, arithmetic and copies ran while one was open for 7% of the time, Pallas kernels for 0%

profile of v1, /device:TPU:8, one launch (start us, length us, event | category | flops | bytes accessed | tf_op | source)
XLA Modules:
  0.0 333.7 jit_solution(9685278580501751007)
XLA Ops:
  1.2 1.2 broadcast_in_dim.10
  3.5 46.9 %all_to_all.10 = bf16[16,5,6144]{2,1,0:T(8,128)(2,1)S(1)} all-to-all(bf16[16,5,6144]{2,1,0:T(8,128)(2,1)S(1)} %reshape.40), channel_id=1, replica_groups=mesh['expert'=16,'fsdp'=16] {'expert'}, dimensions={0} | all-to-all | bytes 1966080 | tf_op jit(solution)/shard_map/all_to_all | solution.py:54
  50.9 1.7 collective-permute-start
  53.0 7.5 %broadcast_in_dim.4 = bf16[1280,6144]{1,0:T(8,128)(2,1)} broadcast(bf16[]{:T(256)} %constant.129.clone.1), dimensions={} | broadcast | bytes 15728642 | tf_op jit(solution)/shard_map/broadcast_in_dim | solution.py:10
  61.6 13.3 %collective-permute-done = bf16[80,6144]{1,0:T(8,128)(2,1)S(1)} collective-permute-done((bf16[80,6144]{1,0:T(8,128)(2,1)S(1)}, bf16[80,6144]{1,0:T(8,128)(2,1)S(1)}, u32[]{:S(2)}, u32[]{:S(2)}) %collective-permute-start) | collective-permute-done | bytes 983072 | tf_op jit(solution)/shard_map/ppermute | solution.py:13
  74.9 1.6 collective-permute-start.2
  76.8 1.7 collective-permute-start.3
  80.6 20.5 %collective-permute-done.2 = bf16[80,6144]{1,0:T(8,128)(2,1)S(1)} collective-permute-done((bf16[80,6144]{1,0:T(8,128)(2,1)S(1)}, bf16[80,6144]{1,0:T(8,128)(2,1)S(1)}, u32[]{:S(2)}, u32[]{:S(2)}) %collective-permute-start.2) | collective-permute-done | bytes 983072 | tf_op jit(solution)/shard_map/ppermute | solution.py:13
  101.1 5.1 %collective-permute-start.5 = (bf16[80,6144]{1,0:T(8,128)(2,1)S(1)}, bf16[80,6144]{1,0:T(8,128)(2,1)S(1)}, u32[]{:S(2)}, u32[]{:S(2)}) collective-permute-start(bf16[80,6144]{1,0:T(8,128)(2,1)S(1)} %collective-permute-done.3), channel_id=1, source_target_pairs={{0,15},{1,0},{2,1},{3,2},{4,3},{5,4},{6,5},{7,6},{8,7},{9,8},{10,9... | collective-permute-start | bytes 2949128 | tf_op jit(solution)/shard_map/ppermute | solution.py:16
  108.2 19.7 %collective-permute-done.4 = bf16[80,6144]{1,0:T(8,128)(2,1)S(1)} collective-permute-done((bf16[80,6144]{1,0:T(8,128)(2,1)S(1)}, bf16[80,6144]{1,0:T(8,128)(2,1)S(1)}, u32[]{:S(2)}, u32[]{:S(2)}) %collective-permute-start.4) | collective-permute-done | bytes 983072 | tf_op jit(solution)/shard_map/ppermute | solution.py:13
  127.9 5.1 %collective-permute-start.7 = (bf16[80,6144]{1,0:T(8,128)(2,1)S(1)}, bf16[80,6144]{1,0:T(8,128)(2,1)S(1)}, u32[]{:S(2)}, u32[]{:S(2)}) collective-permute-start(bf16[80,6144]{1,0:T(8,128)(2,1)S(1)} %collective-permute-done.5), channel_id=1, source_target_pairs={{0,15},{1,0},{2,1},{3,2},{4,3},{5,4},{6,5},{7,6},{8,7},{9,8},{10,9... | collective-permute-start | bytes 2949128 | tf_op jit(solution)/shard_map/ppermute | solution.py:16
  135.0 18.9 %collective-permute-done.6 = bf16[80,6144]{1,0:T(8,128)(2,1)S(1)} collective-permute-done((bf16[80,6144]{1,0:T(8,128)(2,1)S(1)}, bf16[80,6144]{1,0:T(8,128)(2,1)S(1)}, u32[]{:S(2)}, u32[]{:S(2)}) %collective-permute-start.6) | collective-permute-done | bytes 983072 | tf_op jit(solution)/shard_map/ppermute | solution.py:13
  153.9 5.1 %collective-permute-start.9 = (bf16[80,6144]{1,0:T(8,128)(2,1)S(1)}, bf16[80,6144]{1,0:T(8,128)(2,1)S(1)}, u32[]{:S(2)}, u32[]{:S(2)}) collective-permute-start(bf16[80,6144]{1,0:T(8,128)(2,1)S(1)} %collective-permute-done.7), channel_id=1, source_target_pairs={{0,15},{1,0},{2,1},{3,2},{4,3},{5,4},{6,5},{7,6},{8,7},{9,8},{10,9... | collective-permute-start | bytes 2949128 | tf_op jit(solution)/shard_map/ppermute | solution.py:16
  161.0 17.8 %collective-permute-done.8 = bf16[80,6144]{1,0:T(8,128)(2,1)S(1)} collective-permute-done((bf16[80,6144]{1,0:T(8,128)(2,1)S(1)}, bf16[80,6144]{1,0:T(8,128)(2,1)S(1)}, u32[]{:S(2)}, u32[]{:S(2)}) %collective-permute-start.8) | collective-permute-done | bytes 983072 | tf_op jit(solution)/shard_map/ppermute | solution.py:13
  178.9 5.1 %collective-permute-start.11 = (bf16[80,6144]{1,0:T(8,128)(2,1)S(1)}, bf16[80,6144]{1,0:T(8,128)(2,1)S(1)}, u32[]{:S(2)}, u32[]{:S(2)}) collective-permute-start(bf16[80,6144]{1,0:T(8,128)(2,1)S(1)} %collective-permute-done.9), channel_id=1, source_target_pairs={{0,15},{1,0},{2,1},{3,2},{4,3},{5,4},{6,5},{7,6},{8,7},{9,8},{10,9... | collective-permute-start | bytes 2949128 | tf_op jit(solution)/shard_map/ppermute | solution.py:16
  186.0 17.0 %collective-permute-done.10 = bf16[80,6144]{1,0:T(8,128)(2,1)S(1)} collective-permute-done((bf16[80,6144]{1,0:T(8,128)(2,1)S(1)}, bf16[80,6144]{1,0:T(8,128)(2,1)S(1)}, u32[]{:S(2)}, u32[]{:S(2)}) %collective-permute-start.10) | collective-permute-done | bytes 983072 | tf_op jit(solution)/shard_map/ppermute | solution.py:13
  203.0 5.1 %collective-permute-start.13 = (bf16[80,6144]{1,0:T(8,128)(2,1)S(1)}, bf16[80,6144]{1,0:T(8,128)(2,1)S(1)}, u32[]{:S(2)}, u32[]{:S(2)}) collective-permute-start(bf16[80,6144]{1,0:T(8,128)(2,1)S(1)} %collective-permute-done.11), channel_id=1, source_target_pairs={{0,15},{1,0},{2,1},{3,2},{4,3},{5,4},{6,5},{7,6},{8,7},{9,8},{10,9... | collective-permute-start | bytes 2949128 | tf_op jit(solution)/shard_map/ppermute | solution.py:16
  210.1 16.1 %collective-permute-done.12 = bf16[80,6144]{1,0:T(8,128)(2,1)S(1)} collective-permute-done((bf16[80,6144]{1,0:T(8,128)(2,1)S(1)}, bf16[80,6144]{1,0:T(8,128)(2,1)S(1)}, u32[]{:S(2)}, u32[]{:S(2)}) %collective-permute-start.12) | collective-permute-done | bytes 983072 | tf_op jit(solution)/shard_map/ppermute | solution.py:13
  228.3 20.1 %collective-permute-done.14 = bf16[80,6144]{1,0:T(8,128)(2,1)S(1)} collective-permute-done((bf16[80,6144]{1,0:T(8,128)(2,1)S(1)}, bf16[80,6144]{1,0:T(8,128)(2,1)S(1)}, u32[]{:S(2)}, u32[]{:S(2)}) %collective-permute-start.14) | collective-permute-done | bytes 983072 | tf_op jit(solution)/shard_map/ppermute | solution.py:13
  249.5 9.2 %fusion.3 = f32[1280,336]{0,1:T(8,128)S(1)} fusion(bf16[1280,6144]{1,0:T(8,128)(2,1)} %constant_dynamic-update-slice_fusion.15, bf16[1,336,6144]{2,1,0:T(8,128)(2,1)S(1)} %copy-done.2), kind=kOutput, calls=%fused_computation.5 | convolution fusion | flops 5284823040 | bytes 21577728 | tf_op jit(solution)/shard_map/dot_general | solution.py:24
  259.4 15.3 %fusion.8 = bf16[1280,336]{0,1:T(8,128)(2,1)S(1)} fusion(f32[1280,336]{0,1:T(8,128)S(1)} %fusion.3, bf16[1280,6144]{1,0:T(8,128)(2,1)S(1)} %copy-done, bf16[1,336,6144]{2,1,0:T(8,128)(2,1)} %param.9), kind=kOutput, calls=%fused_computation.11 | convolution fusion | flops 5313208320 | bytes 22437888 | tf_op jit(solution)/shard_map/dot_general | solution.py:27
  276.6 1.8 copy.17
  278.4 10.3 %all-to-all-start.1 = ((bf16[256,5,336]{2,1,0:T(8,128)(2,1)}), bf16[256,5,336]{2,1,0:T(8,128)(2,1)S(1)}, u32[]{:S(2)}, u32[]{:S(2)}) async-start(bf16[256,5,336]{2,1,0:T(8,128)(2,1)} %copy.17), calls=%async_computation.1 | async-start | bytes 3145728 | tf_op jit(solution)/shard_map/all_to_all | solution.py:60
  288.9 42.1 %all-to-all-done.1 = bf16[256,5,336]{2,1,0:T(8,128)(2,1)S(1)} async-done(((bf16[256,5,336]{2,1,0:T(8,128)(2,1)}), bf16[256,5,336]{2,1,0:T(8,128)(2,1)S(1)}, u32[]{:S(2)}, u32[]{:S(2)}) %all-to-all-start.1) | async-done | bytes 860192 | tf_op jit(solution)/shard_map/all_to_all | solution.py:60
  (55 shorter events, 25.6 us)
Async XLA Ops:
  50.9 24.0 %collective-permute-start = (bf16[80,6144]{1,0:T(8,128)(2,1)S(1)}, bf16[80,6144]{1,0:T(8,128)(2,1)S(1)}, u32[]{:S(2)}, u32[]{:S(2)}) collective-permute-start(bf16[80,6144]{1,0:T(8,128)(2,1)S(1)} %reshape.41), channel_id=1, source_target_pairs={{0,1},{1,2},{2,3},{3,4},{4,5},{5,6},{6,7},{7,8},{8,9},{9,10},{10,1... | collective-permute-start | bytes 2949128 | tf_op jit(solution)/shard_map/ppermute | solution.py:13
  52.5 24.3 %collective-permute-start.1 = (bf16[80,6144]{1,0:T(8,128)(2,1)S(1)}, bf16[80,6144]{1,0:T(8,128)(2,1)S(1)}, u32[]{:S(2)}, u32[]{:S(2)}) collective-permute-start(bf16[80,6144]{1,0:T(8,128)(2,1)S(1)} %reshape.41), channel_id=1, source_target_pairs={{0,15},{1,0},{2,1},{3,2},{4,3},{5,4},{6,5},{7,6},{8,7},{9,8},{10,9... | collective-permute-start | bytes 2949128 | tf_op jit(solution)/shard_map/ppermute | solution.py:16
  74.9 26.2 %collective-permute-start.2 = (bf16[80,6144]{1,0:T(8,128)(2,1)S(1)}, bf16[80,6144]{1,0:T(8,128)(2,1)S(1)}, u32[]{:S(2)}, u32[]{:S(2)}) collective-permute-start(bf16[80,6144]{1,0:T(8,128)(2,1)S(1)} %collective-permute-done), channel_id=1, source_target_pairs={{0,1},{1,2},{2,3},{3,4},{4,5},{5,6},{6,7},{7,8},{8,9},{9,10},{10,1... | collective-permute-start | bytes 2949128 | tf_op jit(solution)/shard_map/ppermute | solution.py:13
  76.8 24.3 %collective-permute-start.3 = (bf16[80,6144]{1,0:T(8,128)(2,1)S(1)}, bf16[80,6144]{1,0:T(8,128)(2,1)S(1)}, u32[]{:S(2)}, u32[]{:S(2)}) collective-permute-start(bf16[80,6144]{1,0:T(8,128)(2,1)S(1)} %collective-permute-done.1), channel_id=1, source_target_pairs={{0,15},{1,0},{2,1},{3,2},{4,3},{5,4},{6,5},{7,6},{8,7},{9,8},{10,9... | collective-permute-start | bytes 2949128 | tf_op jit(solution)/shard_map/ppermute | solution.py:16
  101.1 26.8 %collective-permute-start.4 = (bf16[80,6144]{1,0:T(8,128)(2,1)S(1)}, bf16[80,6144]{1,0:T(8,128)(2,1)S(1)}, u32[]{:S(2)}, u32[]{:S(2)}) collective-permute-start(bf16[80,6144]{1,0:T(8,128)(2,1)S(1)} %collective-permute-done.2), channel_id=1, source_target_pairs={{0,1},{1,2},{2,3},{3,4},{4,5},{5,6},{6,7},{7,8},{8,9},{9,10},{10,1... | collective-permute-start | bytes 2949128 | tf_op jit(solution)/shard_map/ppermute | solution.py:13
  101.1 26.8 %collective-permute-start.5 = (bf16[80,6144]{1,0:T(8,128)(2,1)S(1)}, bf16[80,6144]{1,0:T(8,128)(2,1)S(1)}, u32[]{:S(2)}, u32[]{:S(2)}) collective-permute-start(bf16[80,6144]{1,0:T(8,128)(2,1)S(1)} %collective-permute-done.3), channel_id=1, source_target_pairs={{0,15},{1,0},{2,1},{3,2},{4,3},{5,4},{6,5},{7,6},{8,7},{9,8},{10,9... | collective-permute-start | bytes 2949128 | tf_op jit(solution)/shard_map/ppermute | solution.py:16
  127.9 25.9 %collective-permute-start.6 = (bf16[80,6144]{1,0:T(8,128)(2,1)S(1)}, bf16[80,6144]{1,0:T(8,128)(2,1)S(1)}, u32[]{:S(2)}, u32[]{:S(2)}) collective-permute-start(bf16[80,6144]{1,0:T(8,128)(2,1)S(1)} %collective-permute-done.4), channel_id=1, source_target_pairs={{0,1},{1,2},{2,3},{3,4},{4,5},{5,6},{6,7},{7,8},{8,9},{9,10},{10,1... | collective-permute-start | bytes 2949128 | tf_op jit(solution)/shard_map/ppermute | solution.py:13
  127.9 25.9 %collective-permute-start.7 = (bf16[80,6144]{1,0:T(8,128)(2,1)S(1)}, bf16[80,6144]{1,0:T(8,128)(2,1)S(1)}, u32[]{:S(2)}, u32[]{:S(2)}) collective-permute-start(bf16[80,6144]{1,0:T(8,128)(2,1)S(1)} %collective-permute-done.5), channel_id=1, source_target_pairs={{0,15},{1,0},{2,1},{3,2},{4,3},{5,4},{6,5},{7,6},{8,7},{9,8},{10,9... | collective-permute-start | bytes 2949128 | tf_op jit(solution)/shard_map/ppermute | solution.py:16
  153.9 25.0 %collective-permute-start.8 = (bf16[80,6144]{1,0:T(8,128)(2,1)S(1)}, bf16[80,6144]{1,0:T(8,128)(2,1)S(1)}, u32[]{:S(2)}, u32[]{:S(2)}) collective-permute-start(bf16[80,6144]{1,0:T(8,128)(2,1)S(1)} %collective-permute-done.6), channel_id=1, source_target_pairs={{0,1},{1,2},{2,3},{3,4},{4,5},{5,6},{6,7},{7,8},{8,9},{9,10},{10,1... | collective-permute-start | bytes 2949128 | tf_op jit(solution)/shard_map/ppermute | solution.py:13
  153.9 25.0 %collective-permute-start.9 = (bf16[80,6144]{1,0:T(8,128)(2,1)S(1)}, bf16[80,6144]{1,0:T(8,128)(2,1)S(1)}, u32[]{:S(2)}, u32[]{:S(2)}) collective-permute-start(bf16[80,6144]{1,0:T(8,128)(2,1)S(1)} %collective-permute-done.7), channel_id=1, source_target_pairs={{0,15},{1,0},{2,1},{3,2},{4,3},{5,4},{6,5},{7,6},{8,7},{9,8},{10,9... | collective-permute-start | bytes 2949128 | tf_op jit(solution)/shard_map/ppermute | solution.py:16
  178.9 24.1 %collective-permute-start.10 = (bf16[80,6144]{1,0:T(8,128)(2,1)S(1)}, bf16[80,6144]{1,0:T(8,128)(2,1)S(1)}, u32[]{:S(2)}, u32[]{:S(2)}) collective-permute-start(bf16[80,6144]{1,0:T(8,128)(2,1)S(1)} %collective-permute-done.8), channel_id=1, source_target_pairs={{0,1},{1,2},{2,3},{3,4},{4,5},{5,6},{6,7},{7,8},{8,9},{9,10},{10,1... | collective-permute-start | bytes 2949128 | tf_op jit(solution)/shard_map/ppermute | solution.py:13
  178.9 24.1 %collective-permute-start.11 = (bf16[80,6144]{1,0:T(8,128)(2,1)S(1)}, bf16[80,6144]{1,0:T(8,128)(2,1)S(1)}, u32[]{:S(2)}, u32[]{:S(2)}) collective-permute-start(bf16[80,6144]{1,0:T(8,128)(2,1)S(1)} %collective-permute-done.9), channel_id=1, source_target_pairs={{0,15},{1,0},{2,1},{3,2},{4,3},{5,4},{6,5},{7,6},{8,7},{9,8},{10,9... | collective-permute-start | bytes 2949128 | tf_op jit(solution)/shard_map/ppermute | solution.py:16
  203.0 23.2 %collective-permute-start.12 = (bf16[80,6144]{1,0:T(8,128)(2,1)S(1)}, bf16[80,6144]{1,0:T(8,128)(2,1)S(1)}, u32[]{:S(2)}, u32[]{:S(2)}) collective-permute-start(bf16[80,6144]{1,0:T(8,128)(2,1)S(1)} %collective-permute-done.10), channel_id=1, source_target_pairs={{0,1},{1,2},{2,3},{3,4},{4,5},{5,6},{6,7},{7,8},{8,9},{9,10},{10,1... | collective-permute-start | bytes 2949128 | tf_op jit(solution)/shard_map/ppermute | solution.py:13
  203.0 24.2 %collective-permute-start.13 = (bf16[80,6144]{1,0:T(8,128)(2,1)S(1)}, bf16[80,6144]{1,0:T(8,128)(2,1)S(1)}, u32[]{:S(2)}, u32[]{:S(2)}) collective-permute-start(bf16[80,6144]{1,0:T(8,128)(2,1)S(1)} %collective-permute-done.11), channel_id=1, source_target_pairs={{0,15},{1,0},{2,1},{3,2},{4,3},{5,4},{6,5},{7,6},{8,7},{9,8},{10,9... | collective-permute-start | bytes 2949128 | tf_op jit(solution)/shard_map/ppermute | solution.py:16
  226.2 22.3 %collective-permute-start.14 = (bf16[80,6144]{1,0:T(8,128)(2,1)S(1)}, bf16[80,6144]{1,0:T(8,128)(2,1)S(1)}, u32[]{:S(2)}, u32[]{:S(2)}) collective-permute-start(bf16[80,6144]{1,0:T(8,128)(2,1)S(1)} %collective-permute-done.12), channel_id=1, source_target_pairs={{0,1},{1,2},{2,3},{3,4},{4,5},{5,6},{6,7},{7,8},{8,9},{9,10},{10,1... | collective-permute-start | bytes 2949128 | tf_op jit(solution)/shard_map/ppermute | solution.py:13
  226.2 23.3 %copy-start.2 = (bf16[1,336,6144]{2,1,0:T(8,128)(2,1)S(1)}, bf16[1,336,6144]{2,1,0:T(8,128)(2,1)}, u32[]{:S(2)}) copy-start(bf16[1,336,6144]{2,1,0:T(8,128)(2,1)} %param.8) | copy-start | bytes 12386308
  249.5 9.9 %copy-start = (bf16[1280,6144]{1,0:T(8,128)(2,1)S(1)}, bf16[1280,6144]{1,0:T(8,128)(2,1)}, u32[]{:S(2)}) copy-start(bf16[1280,6144]{1,0:T(8,128)(2,1)} %constant_dynamic-update-slice_fusion.15) | copy-start | bytes 47185924
  278.4 10.4 %copy-start.1 = (f32[16,4]{0,1:T(4,128)S(1)}, f32[16,4]{0,1:T(4,128)}, u32[]{:S(2)}) copy-start(f32[16,4]{0,1:T(4,128)} %param.7) | copy-start | bytes 772
  278.4 52.6 %all-to-all-start.1 = ((bf16[256,5,336]{2,1,0:T(8,128)(2,1)}), bf16[256,5,336]{2,1,0:T(8,128)(2,1)S(1)}, u32[]{:S(2)}, u32[]{:S(2)}) async-start(bf16[256,5,336]{2,1,0:T(8,128)(2,1)} %copy.17), calls=%async_computation.1 | async-start | bytes 3145728 | tf_op jit(solution)/shard_map/all_to_all | solution.py:60
